TPU v7x, 32 devices: a whole 2x2x4 slice. The times are simulated.
32 devices in a mesh: mol: 2 (over x), occ: 16 (over z, y, core).
Axes of the slice: x: 2, y: 2, z: 4, core: 2. Of those that a mesh axis runs over, the one named last changes fastest.
Arguments:
- integrals: bfloat16 [512, 128, 2048], P(('mol', 'occ')), parts along dimension 0, may hold values from -6 to 6
- orbitals: bfloat16 [4096, 1536], P('mol'), parts along dimension 0
- occ_energy: float32 [256], P('mol'), parts along dimension 0, may hold values from -2 to -0.3
- vir_energy: float32 [3072], P('mol'), parts along dimension 0, may hold values from 0.1 to 3
- owner: int32 [16], P('mol'), parts along dimension 0, may hold values from 0 to 127
- vblock: int32 [16], P('mol'), parts along dimension 0, may hold values from 0 to 7
Outputs:
- factors: bfloat16 [512, 128, 1536], P('mol', 'occ'), parts along dimension 0
- pair_energy: float32 [256, 8], P(('mol', 'occ')), parts along dimension 0
There are 2 independent parts, one for each index of `mol`. A program takes and returns all parts, laid end to end along the dimension named above; each array names one. Nothing has to cross between parts.
Inputs may be any that keep to these rules, and one draw needn't show every extreme that they name: `owner`: each step names one occupied orbital and one virtual block; steps may repeat.
All inputs are finite; a program needn't handle non-finite values.
Results may differ from a plain program's by a relative error of at most 0.001.
Values may be sent and summed in bfloat16 or wider, within the bound.
No kernel may reach another device: no remote copies, remote signals or barrier semaphores. Data moves between devices by JAX's collectives and lax.ppermute only.
A program may use at most 128 MiB of HBM per device.

v0:
```python
import jax
import jax.numpy as jnp
from jax import lax
from jax.sharding import PartitionSpec as P

VBLK = 192
EDGE_PART = 4


def chunk_energies(factors, blocks, occ_rows, occ_cols, vir_chunk, vir_blocks, scale):
    coulomb = lax.dot_general(
        factors, blocks, (((0,), (0,)), ((), ())), preferred_element_type=jnp.float32
    )
    rows_part = vir_chunk[None, :] - occ_rows[:, None]
    cols_part = vir_blocks - occ_cols[:, None]
    denom = rows_part[:, :, None, None] + cols_part[None, None, :, :]
    return jnp.sum(coulomb * coulomb / denom, axis=(1, 3))


def per_device(integrals, orbitals, occ_energy, vir_energy, owner, vblock):
    aux_here, occ_total, basis_count = integrals.shape
    nvir = orbitals.shape[1]
    step_count = owner.shape[0]
    groups = lax.psum(1, "occ")
    local_count = occ_total // groups
    tiles = nvir // 128 if nvir % 128 == 0 else 0
    edge = tiles // EDGE_PART
    if edge >= 1 and tiles - 2 * edge >= 1:
        bounds = [0, edge * 128, nvir - edge * 128, nvir]
    else:
        bounds = [0, nvir]
    chunks = len(bounds) - 1
    ride = step_count == local_count
    rows = integrals.reshape(aux_here, groups, local_count, basis_count)
    rows = jnp.transpose(rows, (1, 0, 2, 3))

    def chunk_product(c):
        return lax.dot_general(
            rows,
            orbitals[:, bounds[c] : bounds[c + 1]],
            (((3,), (0,)), ((), ())),
            preferred_element_type=jnp.float32,
        ).astype(jnp.bfloat16)

    first_product = chunk_product(0)
    first_product, late = lax.optimization_barrier((first_product, owner))
    picked = jnp.take(integrals, late, axis=1)
    picked = (
        jnp.dot(
            picked.reshape(aux_here * step_count, basis_count),
            orbitals,
            preferred_element_type=jnp.float32,
        )
        .astype(jnp.bfloat16)
        .reshape(aux_here, step_count, nvir)
    )
    pieces = jnp.stack(
        [
            lax.dynamic_slice_in_dim(picked[:, s, :], vblock[s] * VBLK, VBLK, axis=1)
            for s in range(step_count)
        ],
        axis=1,
    )
    me = lax.axis_index("occ")
    occ_here = lax.dynamic_slice(occ_energy, (me * local_count,), (local_count,))
    occ_cols = occ_energy[owner]
    vir_blocks = jnp.stack(
        [lax.dynamic_slice(vir_energy, (vblock[s] * VBLK,), (VBLK,)) for s in range(step_count)]
    )
    scale = 1.0 / (aux_here * groups * nvir * VBLK)
    carrier = min(1, chunks - 1) if ride else -1
    if not ride:
        blocks = lax.all_gather(pieces, "occ", axis=0, tiled=True)
    raw = []
    sums = []
    made_at = {}
    pending = []
    for c in range(chunks):
        cols = slice(bounds[c], bounds[c + 1])
        span = bounds[c + 1] - bounds[c]
        product = first_product if c == 0 else chunk_product(c)
        if c == carrier:
            extra = jnp.broadcast_to(pieces[None], (groups, aux_here, step_count, VBLK))
            product = jnp.concatenate([product, extra], axis=3)
        if c >= 1:
            held = (raw[-1],) + tuple(made_at.get(c - 2, ()))
            product, _ = lax.optimization_barrier((product, held))
        got = lax.all_to_all(product, "occ", split_axis=0, concat_axis=0, tiled=True)
        raw.append(got)
        got = got.reshape(groups * aux_here, local_count, got.shape[-1])
        if c == carrier:
            blocks = got[:, :, span:]
            got = got[:, :, :span]
        if c == 0:
            factors = jnp.pad(got, ((0, 0), (0, 0), (0, nvir - span)))
        else:
            factors = lax.dynamic_update_slice(factors, got, (0, 0, bounds[c]))
        if c == carrier:
            whole = raw[-1].reshape(groups * aux_here, local_count, span + VBLK)
            vir_here = jnp.concatenate(
                [vir_energy[cols], jnp.full((VBLK,), jnp.inf, vir_energy.dtype)]
            )
        else:
            whole = lax.optimization_barrier(got)
            vir_here = vir_energy[cols]
        pending.append((whole, vir_here))
        if c >= carrier:
            made = [
                chunk_energies(view, blocks, occ_here, occ_cols, vir_k, vir_blocks, scale)
                for view, vir_k in pending
            ]
            pending = []
            if c < chunks - 1:
                factors, made[0] = lax.optimization_barrier((factors, made[0]))
            made_at[c] = made
            sums.extend(made)
    total = sums[0]
    for extra_sum in sums[1:]:
        total = total + extra_sum
    energies = -total * scale
    return (factors, energies)


def solution(mesh):
    placed = (P(("mol", "occ"), None, None), P("mol", None), P("mol"), P("mol"), P("mol"), P("mol"))
    return jax.shard_map(
        per_device,
        mesh=mesh,
        in_specs=placed,
        out_specs=(P("mol", "occ", None), P(("mol", "occ"), None)),
        check_vma=False,
    )
```

profile of v0, /device:TPU:13, one launch (start us, length us, event | category | flops | bytes accessed | tf_op | source)
XLA Modules:
  0.0 197.3 jit_solution(8760700567116603394)
XLA Ops:
  0.6 0.0 copy-start.5
  0.6 0.0 copy-start.4
  0.6 9.4 %fusion.21 = bf16[16,16,8,384]{3,2,1,0:T(8,128)(2,1)} fusion(bf16[2048,1536]{1,0:T(8,128)(2,1)} %param.7, bf16[16,128,2048]{2,1,0:T(8,128)(2,1)} %param.6), kind=kOutput, calls=%fused_computation.25 | convolution fusion | flops 3222011904 | bytes 11534336 | tf_op jit(solution)/shard_map/dot_general | solution.py:38
  10.1 6.6 %all-to-all-start = ((bf16[16,16,8,384]{3,2,1,0:T(8,128)(2,1)}), bf16[16,16,8,384]{3,2,1,0:T(8,128)(2,1)S(1)}, u32[]{:S(2)}, u32[]{:S(2)}) async-start(bf16[16,16,8,384]{3,2,1,0:T(8,128)(2,1)} %fusion.21), calls=%async_computation | async-start | bytes 3145728 | tf_op jit(solution)/shard_map/all_to_all | solution.py:88
  16.6 0.0 copy-done.4
  16.7 0.7 fusion.42
  22.3 0.0 copy-done.5
  22.4 0.1 broadcast_in_dim.21
  22.5 2.6 %gather_fusion = bf16[8,16,2048]{2,0,1:T(8,128)(2,1)S(1)} fusion(bf16[16,128,2048]{2,1,0:T(8,128)(2,1)} %param.6, s32[1024]{0:T(1024)S(1)} %pad_clamp_fusion.1), kind=kCustom, calls=%fused_computation | custom fusion | bytes 1048608 | tf_op jit(solution)/shard_map/jit(_take)/gather | solution.py:47
  25.2 3.8 %fusion.15 = bf16[16,8,1536]{2,1,0:T(8,128)(2,1)S(1)} fusion(bf16[2048,1536]{1,0:T(8,128)(2,1)} %param.7, bf16[8,16,2048]{2,0,1:T(8,128)(2,1)S(1)} %gather_fusion, pred[128]{0:T(512)(128)(4,1)S(1)} %broadcast_in_dim.21), kind=kOutput, calls=%fused_computation.23 | convolution fusion | flops 805765120 | bytes 7209088 | tf_op jit(solution)/shard_map/dot_general | solution.py:49
  29.0 0.7 fusion.39
  29.7 0.1 constant_dynamic-slice_fusion
  29.8 0.1 constant_dynamic-slice_fusion.1
  29.9 0.1 constant_dynamic-slice_fusion.2
  30.0 0.1 constant_dynamic-slice_fusion.3
  30.1 0.1 constant_dynamic-slice_fusion.4
  30.2 0.1 constant_dynamic-slice_fusion.5
  30.3 0.1 constant_dynamic-slice_fusion.6
  30.4 0.1 constant_dynamic-slice_fusion.7
  30.5 0.2 stack.38
  30.7 10.0 %fusion.16 = bf16[16,16,8,768]{3,2,1,0:T(8,128)(2,1)S(1)} fusion(bf16[2048,1536]{1,0:T(8,128)(2,1)} %param.7, bf16[16,128,2048]{2,1,0:T(8,128)(2,1)} %param.6), kind=kOutput, calls=%fused_computation.24 | convolution fusion | flops 6444023808 | bytes 14680064 | tf_op jit(solution)/shard_map/dot_general | solution.py:38
  40.8 0.1 broadcast_in_dim.25
  40.9 2.6 %pad_maximum_fusion = bf16[16,16,8,960]{3,2,1,0:T(8,128)(2,1)} fusion(bf16[16,16,8,192]{3,2,1,0:T(8,128)(2,1)S(1)} %broadcast_in_dim.25, bf16[16,16,8,768]{3,2,1,0:T(8,128)(2,1)S(1)} %fusion.16), kind=kLoop, calls=%fused_computation.17 | loop fusion | flops 7864320 | bytes 7864320 | tf_op jit(solution)/shard_map/concatenate | solution.py:84
  43.5 9.3 %all-to-all-done = bf16[16,16,8,384]{3,2,1,0:T(8,128)(2,1)S(1)} async-done(((bf16[16,16,8,384]{3,2,1,0:T(8,128)(2,1)}), bf16[16,16,8,384]{3,2,1,0:T(8,128)(2,1)S(1)}, u32[]{:S(2)}, u32[]{:S(2)}) %all-to-all-start) | async-done | bytes 1572896 | tf_op jit(solution)/shard_map/all_to_all | solution.py:88
  52.8 4.9 %all-to-all-start.1 = ((bf16[16,16,8,960]{3,2,1,0:T(8,128)(2,1)}), bf16[16,16,8,960]{3,2,1,0:T(8,128)(2,1)}, u32[]{:S(2)}, u32[]{:S(2)}) async-start(bf16[16,16,8,960]{3,2,1,0:T(8,128)(2,1)} %pad_maximum_fusion), calls=%async_computation.1 | async-start | bytes 8388608 | tf_op jit(solution)/shard_map/all_to_all | solution.py:88
  57.7 0.0 copy-done.3
  57.8 0.0 copy-done
  57.8 0.1 dynamic_slice.59
  57.9 0.6 gather_fusion.1
  58.5 0.1 fusion.41
  58.7 0.1 broadcast_subtract_fusion.3
  58.7 0.1 broadcast_subtract_fusion.1
  58.8 0.1 broadcast_subtract_fusion
  58.9 9.5 %fusion.24 = bf16[16,16,8,384]{3,2,1,0:T(8,128)(2,1)} fusion(bf16[2048,1536]{1,0:T(8,128)(2,1)} %param.7, bf16[16,128,2048]{2,1,0:T(8,128)(2,1)} %param.6), kind=kOutput, calls=%fused_computation.26 | convolution fusion | flops 3222011904 | bytes 11534336 | tf_op jit(solution)/shard_map/dot_general | solution.py:38
  68.4 3.2 %pad.5 = bf16[256,8,1536]{2,1,0:T(8,128)(2,1)} pad(bf16[256,8,384]{2,1,0:T(8,128)(2,1)S(1)} %bitcast.80, bf16[]{:T(256)} %constant.44.clone.1), padding=0_0x0_0x0_1152 | pad | bytes 7864322 | tf_op jit(solution)/shard_map/jit(_pad)/pad | solution.py:95
  71.5 78.7 %all-to-all-done.1 = bf16[16,16,8,960]{3,2,1,0:T(8,128)(2,1)} async-done(((bf16[16,16,8,960]{3,2,1,0:T(8,128)(2,1)}), bf16[16,16,8,960]{3,2,1,0:T(8,128)(2,1)}, u32[]{:S(2)}, u32[]{:S(2)}) %all-to-all-start.1) | async-done | bytes 3932192 | tf_op jit(solution)/shard_map/all_to_all | solution.py:88
  150.2 4.9 %all-to-all-start.2 = ((bf16[16,16,8,384]{3,2,1,0:T(8,128)(2,1)}), bf16[16,16,8,384]{3,2,1,0:T(8,128)(2,1)S(1)}, u32[]{:S(2)}, u32[]{:S(2)}) async-start(bf16[16,16,8,384]{3,2,1,0:T(8,128)(2,1)} %fusion.24), calls=%async_computation.2 | async-start | bytes 3145728 | tf_op jit(solution)/shard_map/all_to_all | solution.py:88
  155.1 2.3 %slice.117 = bf16[256,8,192]{2,1,0:T(8,128)(2,1)} slice(bf16[256,8,960]{2,1,0:T(8,128)(2,1)} %bitcast.18), slice={[0:256], [0:8], [768:960]} | slice | bytes 1572864 | tf_op jit(solution)/shard_map/slice | solution.py:92
  157.4 2.7 %copy.30 = bf16[256,8,192]{0,2,1:T(8,128)(2,1)} copy(bf16[256,8,192]{2,1,0:T(8,128)(2,1)} %slice.117) | data formatting | bytes 1572864
  160.0 3.8 %slice_dynamic-update-slice_fusion = bf16[256,8,1536]{2,1,0:T(8,128)(2,1)} fusion(bf16[256,8,1536]{2,1,0:T(8,128)(2,1)} %pad.5, bf16[256,8,960]{2,1,0:T(8,128)(2,1)} %bitcast.18), kind=kLoop, calls=%fused_computation.19 | loop fusion | bytes 6291456 | tf_op jit(solution)/shard_map/dynamic_update_slice | solution.py:97
  163.9 0.0 copy-done.1
  163.9 4.1 %fusion.1 = f32[8,8]{1,0:T(8,128)S(1)} fusion(f32[8,192]{1,0:T(8,128)S(1)} %broadcast_subtract_fusion.3, f32[8,384]{1,0:T(8,128)S(1)} %get-tuple-element.33, bf16[256,8,384,1]{2,1,0,3:T(8,128)(2,1)S(1)} %bitcast.81, bf16[256,8,192]{0,2,1:T(8,128)(2,1)S(1)} %copy-done.1), kind=kOutput, calls=%fused_computation.6 | convolution fusion | flops 2434793472 | bytes 2377984 | tf_op jit(solution)/shard_map/dot_general | solution.py:11
  168.0 0.0 copy-start.2
  168.0 17.1 %fusion = f32[8,8]{1,0:T(8,128)S(1)} fusion(f32[8,192]{1,0:T(8,128)S(1)} %broadcast_subtract_fusion.3, f32[8,960]{1,0:T(8,128)S(1)} %broadcast_subtract_fusion, bf16[256,8,960,1]{2,1,0,3:T(8,128)(2,1)} %bitcast.32, bf16[256,8,192]{0,2,1:T(8,128)(2,1)S(1)} %copy-done.1), kind=kOutput, calls=%fused_computation.3 | convolution fusion | flops 6086983680 | bytes 4755712 | tf_op jit(solution)/shard_map/dot_general | solution.py:11
  185.1 6.2 %all-to-all-done.2 = bf16[16,16,8,384]{3,2,1,0:T(8,128)(2,1)S(1)} async-done(((bf16[16,16,8,384]{3,2,1,0:T(8,128)(2,1)}), bf16[16,16,8,384]{3,2,1,0:T(8,128)(2,1)S(1)}, u32[]{:S(2)}, u32[]{:S(2)}) %all-to-all-start.2) | async-done | bytes 1572896 | tf_op jit(solution)/shard_map/all_to_all | solution.py:88
  191.3 1.3 constant_dynamic-update-slice_fusion
  192.6 4.1 %fusion.2 = f32[8,8]{1,0:T(8,128)S(1)} fusion(f32[8,384]{1,0:T(8,128)S(1)} %get-tuple-element.32, f32[8,192]{1,0:T(8,128)S(1)} %broadcast_subtract_fusion.3, bf16[256,8,384,1]{2,1,0,3:T(8,128)(2,1)S(1)} %bitcast.79, bf16[256,8,192]{0,2,1:T(8,128)(2,1)S(1)} %copy-done.2), kind=kOutput, calls=%fused_computation.7 | convolution fusion | flops 2434793472 | bytes 2377984 | tf_op jit(solution)/shard_map/dot_general | solution.py:11
  196.7 0.6 negate_multiply_fusion
  (13 shorter events, 0.1 us)
Async XLA Ops:
  0.6 21.7 %copy-start.5 = (s32[8]{0:T(128)S(1)}, s32[8]{0:T(128)}, u32[]{:S(2)}) copy-start(s32[8]{0:T(128)} %param.10) | copy-start | bytes 100
  0.6 16.0 %copy-start.4 = (s32[8]{0:T(128)S(1)}, s32[8]{0:T(128)}, u32[]{:S(2)}) copy-start(s32[8]{0:T(128)} %param.11) | copy-start | bytes 100
  10.1 42.7 %all-to-all-start = ((bf16[16,16,8,384]{3,2,1,0:T(8,128)(2,1)}), bf16[16,16,8,384]{3,2,1,0:T(8,128)(2,1)S(1)}, u32[]{:S(2)}, u32[]{:S(2)}) async-start(bf16[16,16,8,384]{3,2,1,0:T(8,128)(2,1)} %fusion.21), calls=%async_computation | async-start | bytes 3145728 | tf_op jit(solution)/shard_map/all_to_all | solution.py:88
  43.5 14.2 %copy-start.3 = (f32[1536]{0:T(1024)S(1)}, f32[1536]{0:T(1024)}, u32[]{:S(2)}) copy-start(f32[1536]{0:T(1024)} %param.9) | copy-start | bytes 18436
  43.5 14.2 %copy-start = (f32[128]{0:T(128)S(1)}, f32[128]{0:T(128)}, u32[]{:S(2)}) copy-start(f32[128]{0:T(128)} %param.8) | copy-start | bytes 1540
  52.8 97.4 %all-to-all-start.1 = ((bf16[16,16,8,960]{3,2,1,0:T(8,128)(2,1)}), bf16[16,16,8,960]{3,2,1,0:T(8,128)(2,1)}, u32[]{:S(2)}, u32[]{:S(2)}) async-start(bf16[16,16,8,960]{3,2,1,0:T(8,128)(2,1)} %pad_maximum_fusion), calls=%async_computation.1 | async-start | bytes 8388608 | tf_op jit(solution)/shard_map/all_to_all | solution.py:88
  150.2 41.1 %all-to-all-start.2 = ((bf16[16,16,8,384]{3,2,1,0:T(8,128)(2,1)}), bf16[16,16,8,384]{3,2,1,0:T(8,128)(2,1)S(1)}, u32[]{:S(2)}, u32[]{:S(2)}) async-start(bf16[16,16,8,384]{3,2,1,0:T(8,128)(2,1)} %fusion.24), calls=%async_computation.2 | async-start | bytes 3145728 | tf_op jit(solution)/shard_map/all_to_all | solution.py:88
  160.0 3.8 %copy-start.1 = (bf16[256,8,192]{0,2,1:T(8,128)(2,1)S(1)}, bf16[256,8,192]{0,2,1:T(8,128)(2,1)}, u32[]{:S(2)}) copy-start(bf16[256,8,192]{0,2,1:T(8,128)(2,1)} %copy.30) | copy-start | bytes 2359300
  168.0 24.6 %copy-start.2 = (bf16[256,8,192]{0,2,1:T(8,128)(2,1)S(1)}, bf16[256,8,192]{0,2,1:T(8,128)(2,1)}, u32[]{:S(2)}) copy-start(bf16[256,8,192]{0,2,1:T(8,128)(2,1)} %copy.30) | copy-start | bytes 2359300
where the time goes:
time: 198 us; the launch traced here: 197 us
  waiting for transfers between devices  94.2 us (48%)
  matrix products  58.1 us (29%)
  local copies, waits for them, and re-layouts  19.3 us (10%)
  starting transfers between devices  16.4 us (8%)
  between operations  5.89 us (3%)
  other arithmetic  3.46 us (2%)
    all_to_all x3, waiting for transfers between devices, per_device(): lax.all_to_all(product, 'occ', split_axis=0, concat_axis=0, tiled=True)  94.2 us
    dot_general x3, matrix products, chunk_product(): lax.dot_general(rows, orbitals[:, bounds[c]:bounds[c + 1]], (((3,), (0,))...  29 us
    dot_general x3, matrix products, chunk_energies(): lax.dot_general(factors, blocks, (((0,), (0,)), ((), ())), preferred_elem...  25.3 us
    all_to_all x3, starting transfers between devices, per_device(): lax.all_to_all(product, 'occ', split_axis=0, concat_axis=0, tiled=True)  16.4 us
    dynamic_update_slice x2, local copies, waits for them, and re-layouts, per_device(): factors = lax.dynamic_update_slice(factors, got, (0, 0, bounds[c]))  5.13 us
  transfers between devices with their start and end apart: 3, of which 3 were waited for; matrix products, arithmetic and copies ran while one was open for 33% of the time, Pallas kernels for 0%

commit v1 on v0

--- a/solution.py
+++ b/solution.py
@@ -85,7 +85,18 @@
         if c >= 1:
             held = (raw[-1],) + tuple(made_at.get(c - 2, ()))
             product, _ = lax.optimization_barrier((product, held))
-        got = lax.all_to_all(product, "occ", split_axis=0, concat_axis=0, tiled=True)
+        ways, here = (lax.axis_size("occ"), lax.axis_index("occ"))
+        width = product.shape[0] // ways
+        shape = list(product.shape)
+        shape[0] = width
+        height = shape[0]
+        shape[0] = height * ways
+        got = jnp.zeros(shape, product.dtype)
+        for mask in range(ways):
+            part = lax.dynamic_slice_in_dim(product, (here ^ mask) * width, width, axis=0)
+            if mask:
+                part = lax.ppermute(part, "occ", [(d, d ^ mask) for d in range(ways)])
+            got = lax.dynamic_update_slice_in_dim(got, part, (here ^ mask) * height, axis=0)
         raw.append(got)
         got = got.reshape(groups * aux_here, local_count, got.shape[-1])
         if c == carrier:

time: 198 us -> 285 us (1.44)
  starting transfers between devices: 16.4 us -> 62.9 us
  waiting for transfers between devices: 94.2 us -> 126 us
  local copies, waits for them, and re-layouts: 19.3 us -> 23.9 us
  other arithmetic: 3.46 us -> 7.15 us
    ppermute x0 -> x45, waiting for transfers between devices: none -> 126 us  [per_device(): part = lax.ppermute(part, 'occ', [(d, d ^ mask) for d in range(ways)])]
    all_to_all x3 -> x0, waiting for transfers between devices: 94.2 us -> none  [per_device(): lax.all_to_all(product, 'occ', split_axis=0, concat_axis=0, tiled=True)]
    ppermute x0 -> x45, starting transfers between devices: none -> 62.9 us  [per_device(): part = lax.ppermute(part, 'occ', [(d, d ^ mask) for d in range(ways)])]
    all_to_all x3 -> x0, starting transfers between devices: 16.4 us -> none  [per_device(): lax.all_to_all(product, 'occ', split_axis=0, concat_axis=0, tiled=True)]
    dynamic_slice x0 -> x3, local copies, waits for them, and re-layouts: none -> 4.57 us  [per_device(): lax.dynamic_slice_in_dim(product, (here ^ mask) * width, width, axis=0)]
    dynamic_update_slice x2, local copies, waits for them, and re-layouts: 5.13 us -> 0.67 us  [per_device(): factors = lax.dynamic_update_slice(factors, got, (0, 0, bounds[c]))]
    unnamed x13 -> x71, local copies, waits for them, and re-layouts: 2.67 us -> 5.88 us
  transfers between devices with their start and end apart: 3 -> 45, of which waited for: 3 -> 25; matrix products, arithmetic and copies ran while one was open for 33% -> 22% of each run, Pallas kernels for 0% -> 0%
where the time goes in v1:
time: 285 us; the launch traced here: 283 us
  waiting for transfers between devices  126 us (44%)
  starting transfers between devices  62.9 us (22%)
  matrix products  56.8 us (20%)
  local copies, waits for them, and re-layouts  23.9 us (8%)
  other arithmetic  7.15 us (3%)
  between operations  6.76 us (2%)
    ppermute x45, waiting for transfers between devices, per_device(): part = lax.ppermute(part, 'occ', [(d, d ^ mask) for d in range(ways)])  126 us
    ppermute x45, starting transfers between devices, per_device(): part = lax.ppermute(part, 'occ', [(d, d ^ mask) for d in range(ways)])  62.9 us
    dot_general x3, matrix products, chunk_product(): lax.dot_general(rows, orbitals[:, bounds[c]:bounds[c + 1]], (((3,), (0,))...  28.9 us
    dot_general x3, matrix products, chunk_energies(): lax.dot_general(factors, blocks, (((0,), (0,)), ((), ())), preferred_elem...  24.1 us
    unnamed x71, local copies, waits for them, and re-layouts  5.88 us
  transfers between devices with their start and end apart: 45, of which 25 were waited for; matrix products, arithmetic and copies ran while one was open for 22% of the time, Pallas kernels for 0%

profile of v1, /device:TPU:13, one launch (start us, length us, event | category | flops | bytes accessed | tf_op | source)
XLA Modules:
  0.0 283.3 jit_solution(6829553262129051603)
XLA Ops:
  0.7 8.3 %fusion.21 = bf16[16,16,8,384]{3,2,1,0:T(8,128)(2,1)S(1)} fusion(bf16[2048,1536]{1,0:T(8,128)(2,1)} %param.7, bf16[16,128,2048]{2,1,0:T(8,128)(2,1)} %param.6), kind=kOutput, calls=%fused_computation.25 | convolution fusion | flops 3222011904 | bytes 11534336 | tf_op jit(solution)/shard_map/dot_general | solution.py:38
  20.3 11.2 %fusion.16 = bf16[16,16,8,768]{3,2,1,0:T(8,128)(2,1)} fusion(bf16[2048,1536]{1,0:T(8,128)(2,1)} %param.7, bf16[16,128,2048]{2,1,0:T(8,128)(2,1)} %param.6), kind=kOutput, calls=%fused_computation.24 | convolution fusion | flops 6444023808 | bytes 14680064 | tf_op jit(solution)/shard_map/dot_general | solution.py:38
  31.9 9.5 %fusion.24 = bf16[16,16,8,384]{3,2,1,0:T(8,128)(2,1)} fusion(bf16[2048,1536]{1,0:T(8,128)(2,1)} %param.7, bf16[16,128,2048]{2,1,0:T(8,128)(2,1)} %param.6), kind=kOutput, calls=%fused_computation.26 | convolution fusion | flops 3222011904 | bytes 11534336 | tf_op jit(solution)/shard_map/dot_general | solution.py:38
  41.4 2.6 gather_fusion
  44.1 3.8 %fusion.15 = bf16[16,8,1536]{2,1,0:T(8,128)(2,1)S(1)} fusion(bf16[2048,1536]{1,0:T(8,128)(2,1)} %param.7, bf16[8,16,2048]{2,0,1:T(8,128)(2,1)S(1)} %gather_fusion, pred[128]{0:T(512)(128)(4,1)S(1)} %broadcast_in_dim.24), kind=kOutput, calls=%fused_computation.23 | convolution fusion | flops 805765120 | bytes 7209088 | tf_op jit(solution)/shard_map/dot_general | solution.py:49
  49.6 4.6 %pad_maximum_fusion = bf16[16,16,8,960]{3,2,1,0:T(8,128)(2,1)} fusion(bf16[16,16,8,192]{3,2,1,0:T(8,128)(2,1)S(1)} %broadcast_in_dim.50, bf16[16,16,8,768]{3,2,1,0:T(8,128)(2,1)} %fusion.16), kind=kLoop, calls=%fused_computation.17 | loop fusion | flops 7864320 | bytes 7864320 | tf_op jit(solution)/shard_map/concatenate | solution.py:84
  56.5 2.6 collective-permute-start.6
  59.1 2.4 collective-permute-start.7
  62.1 2.3 collective-permute-start.9
  67.1 7.2 %collective-permute-done.7 = bf16[1,16,8,384]{3,2,1,0:T(8,128)(2,1)S(1)} collective-permute-done((bf16[1,16,8,384]{3,2,1,0:T(8,128)(2,1)S(1)}, bf16[1,16,8,384]{3,2,1,0:T(8,128)(2,1)S(1)}, u32[]{:S(2)}, u32[]{:S(2)}) %collective-permute-start.7) | collective-permute-done | bytes 98336 | tf_op jit(solution)/shard_map/ppermute | solution.py:98
  74.3 2.1 collective-permute-done.8
  80.1 4.7 %collective-permute-done.10 = bf16[1,16,8,384]{3,2,1,0:T(8,128)(2,1)S(1)} collective-permute-done((bf16[1,16,8,384]{3,2,1,0:T(8,128)(2,1)S(1)}, bf16[1,16,8,384]{3,2,1,0:T(8,128)(2,1)S(1)}, u32[]{:S(2)}, u32[]{:S(2)}) %collective-permute-start.10) | collective-permute-done | bytes 98336 | tf_op jit(solution)/shard_map/ppermute | solution.py:98
  84.8 4.8 %collective-permute-done.11 = bf16[1,16,8,384]{3,2,1,0:T(8,128)(2,1)S(1)} collective-permute-done((bf16[1,16,8,384]{3,2,1,0:T(8,128)(2,1)S(1)}, bf16[1,16,8,384]{3,2,1,0:T(8,128)(2,1)S(1)}, u32[]{:S(2)}, u32[]{:S(2)}) %collective-permute-start.11) | collective-permute-done | bytes 98336 | tf_op jit(solution)/shard_map/ppermute | solution.py:98
  89.7 2.1 collective-permute-done.12
  91.8 2.0 collective-permute-done.13
  93.8 2.1 collective-permute-done.14
  98.2 2.0 copy-done.2
  103.3 1.7 collective-permute-start.19
  105.0 3.6 %pad.5 = bf16[256,8,1536]{2,1,0:T(8,128)(2,1)} pad(bf16[256,8,384]{2,1,0:T(8,128)(2,1)S(1)} %bitcast.85, bf16[]{:T(256)} %constant.29.clone.1), padding=0_0x0_0x0_1152 | pad | bytes 7864322 | tf_op jit(solution)/shard_map/jit(_pad)/pad | solution.py:106
  110.4 2.0 collective-permute-start.21
  112.4 3.1 %collective-permute-done.17 = bf16[1,16,8,960]{3,2,1,0:T(8,128)(2,1)S(1)} collective-permute-done((bf16[1,16,8,960]{3,2,1,0:T(8,128)(2,1)}, bf16[1,16,8,960]{3,2,1,0:T(8,128)(2,1)S(1)}, u32[]{:S(2)}, u32[]{:S(2)}) %collective-permute-start.17) | collective-permute-done | bytes 245792 | tf_op jit(solution)/shard_map/ppermute | solution.py:98
  115.6 2.5 collective-permute-start.23
  118.1 1.8 collective-permute-start.24
  119.9 12.5 %collective-permute-done.20 = bf16[1,16,8,960]{3,2,1,0:T(8,128)(2,1)S(1)} collective-permute-done((bf16[1,16,8,960]{3,2,1,0:T(8,128)(2,1)S(1)}, bf16[1,16,8,960]{3,2,1,0:T(8,128)(2,1)S(1)}, u32[]{:S(2)}, u32[]{:S(2)}) %collective-permute-start.20) | collective-permute-done | bytes 245792 | tf_op jit(solution)/shard_map/ppermute | solution.py:98
  132.5 4.8 %collective-permute-start.25 = (bf16[1,16,8,960]{3,2,1,0:T(8,128)(2,1)S(1)}, bf16[1,16,8,960]{3,2,1,0:T(8,128)(2,1)S(1)}, u32[]{:S(2)}, u32[]{:S(2)}) collective-permute-start(bf16[1,16,8,960]{3,2,1,0:T(8,128)(2,1)S(1)} %get-tuple-element.18), channel_id=1, source_target_pairs={{0,11},{1,10},{2,9},{3,8},{4,15},{5,14},{6,13},{7,12},{8,3},{9,2},... | collective-permute-start | bytes 737288 | tf_op jit(solution)/shard_map/ppermute | solution.py:98
  142.9 29.4 %collective-permute-done.24 = bf16[1,16,8,960]{3,2,1,0:T(8,128)(2,1)S(1)} collective-permute-done((bf16[1,16,8,960]{3,2,1,0:T(8,128)(2,1)S(1)}, bf16[1,16,8,960]{3,2,1,0:T(8,128)(2,1)S(1)}, u32[]{:S(2)}, u32[]{:S(2)}) %collective-permute-start.24) | collective-permute-done | bytes 245792 | tf_op jit(solution)/shard_map/ppermute | solution.py:98
  172.3 2.8 collective-permute-start.29
  175.1 2.8 collective-permute-done.25
  177.9 13.2 %collective-permute-done.26 = bf16[1,16,8,960]{3,2,1,0:T(8,128)(2,1)S(1)} collective-permute-done((bf16[1,16,8,960]{3,2,1,0:T(8,128)(2,1)S(1)}, bf16[1,16,8,960]{3,2,1,0:T(8,128)(2,1)S(1)}, u32[]{:S(2)}, u32[]{:S(2)}) %collective-permute-start.26) | collective-permute-done | bytes 245792 | tf_op jit(solution)/shard_map/ppermute | solution.py:98
  191.1 5.6 %collective-permute-done.27 = bf16[1,16,8,960]{3,2,1,0:T(8,128)(2,1)S(1)} collective-permute-done((bf16[1,16,8,960]{3,2,1,0:T(8,128)(2,1)S(1)}, bf16[1,16,8,960]{3,2,1,0:T(8,128)(2,1)S(1)}, u32[]{:S(2)}, u32[]{:S(2)}) %collective-permute-start.27) | collective-permute-done | bytes 245792 | tf_op jit(solution)/shard_map/ppermute | solution.py:98
  196.8 6.9 %collective-permute-done.28 = bf16[1,16,8,960]{3,2,1,0:T(8,128)(2,1)S(1)} collective-permute-done((bf16[1,16,8,960]{3,2,1,0:T(8,128)(2,1)S(1)}, bf16[1,16,8,960]{3,2,1,0:T(8,128)(2,1)S(1)}, u32[]{:S(2)}, u32[]{:S(2)}) %collective-permute-start.28) | collective-permute-done | bytes 245792 | tf_op jit(solution)/shard_map/ppermute | solution.py:98
  203.7 5.6 %collective-permute-done.29 = bf16[1,16,8,960]{3,2,1,0:T(8,128)(2,1)S(1)} collective-permute-done((bf16[1,16,8,960]{3,2,1,0:T(8,128)(2,1)S(1)}, bf16[1,16,8,960]{3,2,1,0:T(8,128)(2,1)S(1)}, u32[]{:S(2)}, u32[]{:S(2)}) %collective-permute-start.29) | collective-permute-done | bytes 245792 | tf_op jit(solution)/shard_map/ppermute | solution.py:98
  209.5 1.8 copy-done.4
  211.4 1.7 copy.31
  213.4 1.9 constant_dynamic-slice_fusion.52
  215.7 1.8 collective-permute-start.32
  217.5 1.7 collective-permute-start.34
  219.2 15.9 %fusion = f32[8,8]{1,0:T(8,128)S(1)} fusion(f32[8,192]{1,0:T(8,128)S(1)} %broadcast_subtract_fusion.3, f32[8,960]{1,0:T(8,128)S(1)} %copy-done.20, bf16[256,8,960,1]{2,1,0,3:T(8,128)(2,1)S(1)} %bitcast.79, bf16[256,8,192]{0,2,1:T(8,128)(2,1)} %copy.31), kind=kOutput, calls=%fused_computation.3 | convolution fusion | flops 6086983680 | bytes 4755712 | tf_op jit(solution)/shard_map/dot_general | solution.py:11
  235.1 4.1 %fusion.1 = f32[8,8]{1,0:T(8,128)S(1)} fusion(f32[8,192]{1,0:T(8,128)S(1)} %broadcast_subtract_fusion.3, f32[8,384]{1,0:T(8,128)S(1)} %copy-done.23, bf16[256,8,384,1]{2,1,0,3:T(8,128)(2,1)S(1)} %bitcast.86, bf16[256,8,192]{0,2,1:T(8,128)(2,1)S(1)} %copy-done.9), kind=kOutput, calls=%fused_computation.6 | convolution fusion | flops 2434793472 | bytes 2377984 | tf_op jit(solution)/shard_map/dot_general | solution.py:11
  239.8 2.7 collective-permute-start.36
  242.7 2.6 collective-permute-start.38
  245.4 3.6 %collective-permute-start.40 = (bf16[1,16,8,384]{3,2,1,0:T(8,128)(2,1)S(1)}, bf16[1,16,8,384]{3,2,1,0:T(8,128)(2,1)S(1)}, u32[]{:S(2)}, u32[]{:S(2)}) collective-permute-start(bf16[1,16,8,384]{3,2,1,0:T(8,128)(2,1)S(1)} %get-tuple-element.34), channel_id=1, source_target_pairs={{0,11},{1,10},{2,9},{3,8},{4,15},{5,14},{6,13},{7,12},{8,3},{9,2},... | collective-permute-start | bytes 294920 | tf_op jit(solution)/shard_map/ppermute | solution.py:98
  249.2 8.3 %collective-permute-start.42 = (bf16[1,16,8,384]{3,2,1,0:T(8,128)(2,1)S(1)}, bf16[1,16,8,384]{3,2,1,0:T(8,128)(2,1)S(1)}, u32[]{:S(2)}, u32[]{:S(2)}) collective-permute-start(bf16[1,16,8,384]{3,2,1,0:T(8,128)(2,1)S(1)} %get-tuple-element.32), channel_id=1, source_target_pairs={{0,13},{1,12},{2,15},{3,14},{4,9},{5,8},{6,11},{7,10},{8,5},{9,4},... | collective-permute-start | bytes 294920 | tf_op jit(solution)/shard_map/ppermute | solution.py:98
  259.3 2.9 %collective-permute-done.39 = bf16[1,16,8,384]{3,2,1,0:T(8,128)(2,1)S(1)} collective-permute-done((bf16[1,16,8,384]{3,2,1,0:T(8,128)(2,1)S(1)}, bf16[1,16,8,384]{3,2,1,0:T(8,128)(2,1)S(1)}, u32[]{:S(2)}, u32[]{:S(2)}) %collective-permute-start.39) | collective-permute-done | bytes 98336 | tf_op jit(solution)/shard_map/ppermute | solution.py:98
  264.3 7.9 %collective-permute-done.41 = bf16[1,16,8,384]{3,2,1,0:T(8,128)(2,1)S(1)} collective-permute-done((bf16[1,16,8,384]{3,2,1,0:T(8,128)(2,1)S(1)}, bf16[1,16,8,384]{3,2,1,0:T(8,128)(2,1)S(1)}, u32[]{:S(2)}, u32[]{:S(2)}) %collective-permute-start.41) | collective-permute-done | bytes 98336 | tf_op jit(solution)/shard_map/ppermute | solution.py:98
  272.2 2.4 collective-permute-done.42
  275.8 2.4 collective-permute-done.44
  278.6 4.1 %fusion.2 = f32[8,8]{1,0:T(8,128)S(1)} fusion(f32[8,384]{1,0:T(8,128)S(1)} %get-tuple-element.80, f32[8,192]{1,0:T(8,128)S(1)} %broadcast_subtract_fusion.3, bf16[256,8,384,1]{2,1,0,3:T(8,128)(2,1)S(1)} %bitcast.82, bf16[256,8,192]{0,2,1:T(8,128)(2,1)S(1)} %copy-done.9), kind=kOutput, calls=%fused_computation.7 | convolution fusion | flops 2434793472 | bytes 2377984 | tf_op jit(solution)/shard_map/dot_general | solution.py:11
  (204 shorter events, 38.2 us)
Async XLA Ops:
  10.4 46.0 %collective-permute-start = (bf16[1,16,8,384]{3,2,1,0:T(8,128)(2,1)}, bf16[1,16,8,384]{3,2,1,0:T(8,128)(2,1)S(1)}, u32[]{:S(2)}, u32[]{:S(2)}) collective-permute-start(bf16[1,16,8,384]{3,2,1,0:T(8,128)(2,1)} %get-tuple-element.60), channel_id=1, source_target_pairs={{0,1},{1,0},{2,3},{3,2},{4,5},{5,4},{6,7},{7,6},{8,9},{9,8},{10,11... | collective-permute-start | bytes 294920 | tf_op jit(solution)/shard_map/ppermute | solution.py:98
  11.1 45.4 %collective-permute-start.1 = (bf16[1,16,8,384]{3,2,1,0:T(8,128)(2,1)}, bf16[1,16,8,384]{3,2,1,0:T(8,128)(2,1)S(1)}, u32[]{:S(2)}, u32[]{:S(2)}) collective-permute-start(bf16[1,16,8,384]{3,2,1,0:T(8,128)(2,1)} %get-tuple-element.59), channel_id=1, source_target_pairs={{0,2},{1,3},{2,0},{3,1},{4,6},{5,7},{6,4},{7,5},{8,10},{9,11},{10,... | collective-permute-start | bytes 294920 | tf_op jit(solution)/shard_map/ppermute | solution.py:98
  11.3 47.8 %collective-permute-start.2 = (bf16[1,16,8,384]{3,2,1,0:T(8,128)(2,1)}, bf16[1,16,8,384]{3,2,1,0:T(8,128)(2,1)S(1)}, u32[]{:S(2)}, u32[]{:S(2)}) collective-permute-start(bf16[1,16,8,384]{3,2,1,0:T(8,128)(2,1)} %get-tuple-element.58), channel_id=1, source_target_pairs={{0,3},{1,2},{2,1},{3,0},{4,7},{5,6},{6,5},{7,4},{8,11},{9,10},{10,... | collective-permute-start | bytes 294920 | tf_op jit(solution)/shard_map/ppermute | solution.py:98
  12.7 48.8 %collective-permute-start.3 = (bf16[1,16,8,384]{3,2,1,0:T(8,128)(2,1)}, bf16[1,16,8,384]{3,2,1,0:T(8,128)(2,1)S(1)}, u32[]{:S(2)}, u32[]{:S(2)}) collective-permute-start(bf16[1,16,8,384]{3,2,1,0:T(8,128)(2,1)} %get-tuple-element.57), channel_id=1, source_target_pairs={{0,4},{1,5},{2,6},{3,7},{4,0},{5,1},{6,2},{7,3},{8,12},{9,13},{10,... | collective-permute-start | bytes 294920 | tf_op jit(solution)/shard_map/ppermute | solution.py:98
  12.9 49.2 %collective-permute-start.4 = (bf16[1,16,8,384]{3,2,1,0:T(8,128)(2,1)}, bf16[1,16,8,384]{3,2,1,0:T(8,128)(2,1)S(1)}, u32[]{:S(2)}, u32[]{:S(2)}) collective-permute-start(bf16[1,16,8,384]{3,2,1,0:T(8,128)(2,1)} %get-tuple-element.56), channel_id=1, source_target_pairs={{0,5},{1,4},{2,7},{3,6},{4,1},{5,0},{6,3},{7,2},{8,13},{9,12},{10,... | collective-permute-start | bytes 294920 | tf_op jit(solution)/shard_map/ppermute | solution.py:98
  56.3 8.1 %collective-permute-start.5 = (bf16[1,16,8,384]{3,2,1,0:T(8,128)(2,1)S(1)}, bf16[1,16,8,384]{3,2,1,0:T(8,128)(2,1)S(1)}, u32[]{:S(2)}, u32[]{:S(2)}) collective-permute-start(bf16[1,16,8,384]{3,2,1,0:T(8,128)(2,1)S(1)} %copy-done.19), channel_id=1, source_target_pairs={{0,6},{1,7},{2,4},{3,5},{4,2},{5,3},{6,0},{7,1},{8,14},{9,15},{10,... | collective-permute-start | bytes 294920 | tf_op jit(solution)/shard_map/ppermute | solution.py:98
  56.5 9.3 %collective-permute-start.6 = (bf16[1,16,8,384]{3,2,1,0:T(8,128)(2,1)S(1)}, bf16[1,16,8,384]{3,2,1,0:T(8,128)(2,1)S(1)}, u32[]{:S(2)}, u32[]{:S(2)}) collective-permute-start(bf16[1,16,8,384]{3,2,1,0:T(8,128)(2,1)S(1)} %copy-done.18), channel_id=1, source_target_pairs={{0,7},{1,6},{2,5},{3,4},{4,3},{5,2},{6,1},{7,0},{8,15},{9,14},{10,... | collective-permute-start | bytes 294920 | tf_op jit(solution)/shard_map/ppermute | solution.py:98
  59.1 15.2 %collective-permute-start.7 = (bf16[1,16,8,384]{3,2,1,0:T(8,128)(2,1)S(1)}, bf16[1,16,8,384]{3,2,1,0:T(8,128)(2,1)S(1)}, u32[]{:S(2)}, u32[]{:S(2)}) collective-permute-start(bf16[1,16,8,384]{3,2,1,0:T(8,128)(2,1)S(1)} %copy-done.17), channel_id=1, source_target_pairs={{0,8},{1,9},{2,10},{3,11},{4,12},{5,13},{6,14},{7,15},{8,0},{9,1},... | collective-permute-start | bytes 294920 | tf_op jit(solution)/shard_map/ppermute | solution.py:98
  61.5 14.9 %collective-permute-start.8 = (bf16[1,16,8,384]{3,2,1,0:T(8,128)(2,1)S(1)}, bf16[1,16,8,384]{3,2,1,0:T(8,128)(2,1)S(1)}, u32[]{:S(2)}, u32[]{:S(2)}) collective-permute-start(bf16[1,16,8,384]{3,2,1,0:T(8,128)(2,1)S(1)} %copy-done.16), channel_id=1, source_target_pairs={{0,9},{1,8},{2,11},{3,10},{4,13},{5,12},{6,15},{7,14},{8,1},{9,0},... | collective-permute-start | bytes 294920 | tf_op jit(solution)/shard_map/ppermute | solution.py:98
  62.1 34.4 %copy-start.1 = (bf16[16,16,8,960]{3,2,1,0:T(8,128)(2,1)S(1)}, bf16[16,16,8,960]{3,2,1,0:T(8,128)(2,1)}, u32[]{:S(2)}) copy-start(bf16[16,16,8,960]{3,2,1,0:T(8,128)(2,1)} %pad_maximum_fusion) | copy-start | bytes 11796484
  62.1 16.4 %collective-permute-start.9 = (bf16[1,16,8,384]{3,2,1,0:T(8,128)(2,1)S(1)}, bf16[1,16,8,384]{3,2,1,0:T(8,128)(2,1)S(1)}, u32[]{:S(2)}, u32[]{:S(2)}) collective-permute-start(bf16[1,16,8,384]{3,2,1,0:T(8,128)(2,1)S(1)} %copy-done.15), channel_id=1, source_target_pairs={{0,10},{1,11},{2,8},{3,9},{4,14},{5,15},{6,12},{7,13},{8,2},{9,3},... | collective-permute-start | bytes 294920 | tf_op jit(solution)/shard_map/ppermute | solution.py:98
  64.4 20.4 %collective-permute-start.10 = (bf16[1,16,8,384]{3,2,1,0:T(8,128)(2,1)S(1)}, bf16[1,16,8,384]{3,2,1,0:T(8,128)(2,1)S(1)}, u32[]{:S(2)}, u32[]{:S(2)}) collective-permute-start(bf16[1,16,8,384]{3,2,1,0:T(8,128)(2,1)S(1)} %copy-done.14), channel_id=1, source_target_pairs={{0,11},{1,10},{2,9},{3,8},{4,15},{5,14},{6,13},{7,12},{8,3},{9,2},... | collective-permute-start | bytes 294920 | tf_op jit(solution)/shard_map/ppermute | solution.py:98
  65.8 23.9 %collective-permute-start.11 = (bf16[1,16,8,384]{3,2,1,0:T(8,128)(2,1)S(1)}, bf16[1,16,8,384]{3,2,1,0:T(8,128)(2,1)S(1)}, u32[]{:S(2)}, u32[]{:S(2)}) collective-permute-start(bf16[1,16,8,384]{3,2,1,0:T(8,128)(2,1)S(1)} %get-tuple-element.49), channel_id=1, source_target_pairs={{0,12},{1,13},{2,14},{3,15},{4,8},{5,9},{6,10},{7,11},{8,4},{9,5},... | collective-permute-start | bytes 294920 | tf_op jit(solution)/shard_map/ppermute | solution.py:98
  74.3 17.5 %collective-permute-start.12 = (bf16[1,16,8,384]{3,2,1,0:T(8,128)(2,1)S(1)}, bf16[1,16,8,384]{3,2,1,0:T(8,128)(2,1)S(1)}, u32[]{:S(2)}, u32[]{:S(2)}) collective-permute-start(bf16[1,16,8,384]{3,2,1,0:T(8,128)(2,1)S(1)} %get-tuple-element.48), channel_id=1, source_target_pairs={{0,13},{1,12},{2,15},{3,14},{4,9},{5,8},{6,11},{7,10},{8,5},{9,4},... | collective-permute-start | bytes 294920 | tf_op jit(solution)/shard_map/ppermute | solution.py:98
  76.4 17.4 %collective-permute-start.13 = (bf16[1,16,8,384]{3,2,1,0:T(8,128)(2,1)S(1)}, bf16[1,16,8,384]{3,2,1,0:T(8,128)(2,1)S(1)}, u32[]{:S(2)}, u32[]{:S(2)}) collective-permute-start(bf16[1,16,8,384]{3,2,1,0:T(8,128)(2,1)S(1)} %get-tuple-element.47), channel_id=1, source_target_pairs={{0,14},{1,15},{2,12},{3,13},{4,10},{5,11},{6,8},{7,9},{8,6},{9,7},... | collective-permute-start | bytes 294920 | tf_op jit(solution)/shard_map/ppermute | solution.py:98
  78.5 17.4 %collective-permute-start.14 = (bf16[1,16,8,384]{3,2,1,0:T(8,128)(2,1)S(1)}, bf16[1,16,8,384]{3,2,1,0:T(8,128)(2,1)S(1)}, u32[]{:S(2)}, u32[]{:S(2)}) collective-permute-start(bf16[1,16,8,384]{3,2,1,0:T(8,128)(2,1)S(1)} %get-tuple-element.46), channel_id=1, source_target_pairs={{0,15},{1,14},{2,13},{3,12},{4,11},{5,10},{6,9},{7,8},{8,7},{9,6},... | collective-permute-start | bytes 294920 | tf_op jit(solution)/shard_map/ppermute | solution.py:98
  100.2 8.5 %collective-permute-start.15 = (bf16[1,16,8,960]{3,2,1,0:T(8,128)(2,1)}, bf16[1,16,8,960]{3,2,1,0:T(8,128)(2,1)}, u32[]{:S(2)}, u32[]{:S(2)}) collective-permute-start(bf16[1,16,8,960]{3,2,1,0:T(8,128)(2,1)} %get-tuple-element.28), channel_id=1, source_target_pairs={{0,1},{1,0},{2,3},{3,2},{4,5},{5,4},{6,7},{7,6},{8,9},{9,8},{10,11... | collective-permute-start | bytes 737288 | tf_op jit(solution)/shard_map/ppermute | solution.py:98
  101.3 9.0 %collective-permute-start.16 = (bf16[1,16,8,960]{3,2,1,0:T(8,128)(2,1)}, bf16[1,16,8,960]{3,2,1,0:T(8,128)(2,1)S(1)}, u32[]{:S(2)}, u32[]{:S(2)}) collective-permute-start(bf16[1,16,8,960]{3,2,1,0:T(8,128)(2,1)} %get-tuple-element.27), channel_id=1, source_target_pairs={{0,2},{1,3},{2,0},{3,1},{4,6},{5,7},{6,4},{7,5},{8,10},{9,11},{10,... | collective-permute-start | bytes 737288 | tf_op jit(solution)/shard_map/ppermute | solution.py:98
  102.7 12.9 %collective-permute-start.17 = (bf16[1,16,8,960]{3,2,1,0:T(8,128)(2,1)}, bf16[1,16,8,960]{3,2,1,0:T(8,128)(2,1)S(1)}, u32[]{:S(2)}, u32[]{:S(2)}) collective-permute-start(bf16[1,16,8,960]{3,2,1,0:T(8,128)(2,1)} %get-tuple-element.26), channel_id=1, source_target_pairs={{0,3},{1,2},{2,1},{3,0},{4,7},{5,6},{6,5},{7,4},{8,11},{9,10},{10,... | collective-permute-start | bytes 737288 | tf_op jit(solution)/shard_map/ppermute | solution.py:98
  103.3 12.3 %collective-permute-start.18 = (bf16[1,16,8,960]{3,2,1,0:T(8,128)(2,1)}, bf16[1,16,8,960]{3,2,1,0:T(8,128)(2,1)S(1)}, u32[]{:S(2)}, u32[]{:S(2)}) collective-permute-start(bf16[1,16,8,960]{3,2,1,0:T(8,128)(2,1)} %get-tuple-element.25), channel_id=1, source_target_pairs={{0,4},{1,5},{2,6},{3,7},{4,0},{5,1},{6,2},{7,3},{8,12},{9,13},{10,... | collective-permute-start | bytes 737288 | tf_op jit(solution)/shard_map/ppermute | solution.py:98
  103.3 14.8 %collective-permute-start.19 = (bf16[1,16,8,960]{3,2,1,0:T(8,128)(2,1)}, bf16[1,16,8,960]{3,2,1,0:T(8,128)(2,1)S(1)}, u32[]{:S(2)}, u32[]{:S(2)}) collective-permute-start(bf16[1,16,8,960]{3,2,1,0:T(8,128)(2,1)} %get-tuple-element.24), channel_id=1, source_target_pairs={{0,5},{1,4},{2,7},{3,6},{4,1},{5,0},{6,3},{7,2},{8,13},{9,12},{10,... | collective-permute-start | bytes 737288 | tf_op jit(solution)/shard_map/ppermute | solution.py:98
  108.7 23.8 %collective-permute-start.20 = (bf16[1,16,8,960]{3,2,1,0:T(8,128)(2,1)S(1)}, bf16[1,16,8,960]{3,2,1,0:T(8,128)(2,1)S(1)}, u32[]{:S(2)}, u32[]{:S(2)}) collective-permute-start(bf16[1,16,8,960]{3,2,1,0:T(8,128)(2,1)S(1)} %copy-done.13), channel_id=1, source_target_pairs={{0,6},{1,7},{2,4},{3,5},{4,2},{5,3},{6,0},{7,1},{8,14},{9,15},{10,... | collective-permute-start | bytes 737288 | tf_op jit(solution)/shard_map/ppermute | solution.py:98
  110.4 27.7 %collective-permute-start.21 = (bf16[1,16,8,960]{3,2,1,0:T(8,128)(2,1)S(1)}, bf16[1,16,8,960]{3,2,1,0:T(8,128)(2,1)S(1)}, u32[]{:S(2)}, u32[]{:S(2)}) collective-permute-start(bf16[1,16,8,960]{3,2,1,0:T(8,128)(2,1)S(1)} %copy-done.12), channel_id=1, source_target_pairs={{0,7},{1,6},{2,5},{3,4},{4,3},{5,2},{6,1},{7,0},{8,15},{9,14},{10,... | collective-permute-start | bytes 737288 | tf_op jit(solution)/shard_map/ppermute | solution.py:98
  115.6 24.1 %collective-permute-start.22 = (bf16[1,16,8,960]{3,2,1,0:T(8,128)(2,1)S(1)}, bf16[1,16,8,960]{3,2,1,0:T(8,128)(2,1)S(1)}, u32[]{:S(2)}, u32[]{:S(2)}) collective-permute-start(bf16[1,16,8,960]{3,2,1,0:T(8,128)(2,1)S(1)} %copy-done.11), channel_id=1, source_target_pairs={{0,8},{1,9},{2,10},{3,11},{4,12},{5,13},{6,14},{7,15},{8,0},{9,1},... | collective-permute-start | bytes 737288 | tf_op jit(solution)/shard_map/ppermute | solution.py:98
  115.6 25.7 %collective-permute-start.23 = (bf16[1,16,8,960]{3,2,1,0:T(8,128)(2,1)S(1)}, bf16[1,16,8,960]{3,2,1,0:T(8,128)(2,1)S(1)}, u32[]{:S(2)}, u32[]{:S(2)}) collective-permute-start(bf16[1,16,8,960]{3,2,1,0:T(8,128)(2,1)S(1)} %copy-done.10), channel_id=1, source_target_pairs={{0,9},{1,8},{2,11},{3,10},{4,13},{5,12},{6,15},{7,14},{8,1},{9,0},... | collective-permute-start | bytes 737288 | tf_op jit(solution)/shard_map/ppermute | solution.py:98
  118.1 54.2 %collective-permute-start.24 = (bf16[1,16,8,960]{3,2,1,0:T(8,128)(2,1)S(1)}, bf16[1,16,8,960]{3,2,1,0:T(8,128)(2,1)S(1)}, u32[]{:S(2)}, u32[]{:S(2)}) collective-permute-start(bf16[1,16,8,960]{3,2,1,0:T(8,128)(2,1)S(1)} %get-tuple-element.19), channel_id=1, source_target_pairs={{0,10},{1,11},{2,8},{3,9},{4,14},{5,15},{6,12},{7,13},{8,2},{9,3},... | collective-permute-start | bytes 737288 | tf_op jit(solution)/shard_map/ppermute | solution.py:98
  132.5 45.4 %collective-permute-start.25 = (bf16[1,16,8,960]{3,2,1,0:T(8,128)(2,1)S(1)}, bf16[1,16,8,960]{3,2,1,0:T(8,128)(2,1)S(1)}, u32[]{:S(2)}, u32[]{:S(2)}) collective-permute-start(bf16[1,16,8,960]{3,2,1,0:T(8,128)(2,1)S(1)} %get-tuple-element.18), channel_id=1, source_target_pairs={{0,11},{1,10},{2,9},{3,8},{4,15},{5,14},{6,13},{7,12},{8,3},{9,2},... | collective-permute-start | bytes 737288 | tf_op jit(solution)/shard_map/ppermute | solution.py:98
  138.1 53.0 %collective-permute-start.26 = (bf16[1,16,8,960]{3,2,1,0:T(8,128)(2,1)S(1)}, bf16[1,16,8,960]{3,2,1,0:T(8,128)(2,1)S(1)}, u32[]{:S(2)}, u32[]{:S(2)}) collective-permute-start(bf16[1,16,8,960]{3,2,1,0:T(8,128)(2,1)S(1)} %get-tuple-element.17), channel_id=1, source_target_pairs={{0,12},{1,13},{2,14},{3,15},{4,8},{5,9},{6,10},{7,11},{8,4},{9,5},... | collective-permute-start | bytes 737288 | tf_op jit(solution)/shard_map/ppermute | solution.py:98
  139.6 57.1 %collective-permute-start.27 = (bf16[1,16,8,960]{3,2,1,0:T(8,128)(2,1)S(1)}, bf16[1,16,8,960]{3,2,1,0:T(8,128)(2,1)S(1)}, u32[]{:S(2)}, u32[]{:S(2)}) collective-permute-start(bf16[1,16,8,960]{3,2,1,0:T(8,128)(2,1)S(1)} %get-tuple-element.16), channel_id=1, source_target_pairs={{0,13},{1,12},{2,15},{3,14},{4,9},{5,8},{6,11},{7,10},{8,5},{9,4},... | collective-permute-start | bytes 737288 | tf_op jit(solution)/shard_map/ppermute | solution.py:98
  141.3 62.4 %collective-permute-start.28 = (bf16[1,16,8,960]{3,2,1,0:T(8,128)(2,1)S(1)}, bf16[1,16,8,960]{3,2,1,0:T(8,128)(2,1)S(1)}, u32[]{:S(2)}, u32[]{:S(2)}) collective-permute-start(bf16[1,16,8,960]{3,2,1,0:T(8,128)(2,1)S(1)} %get-tuple-element.15), channel_id=1, source_target_pairs={{0,14},{1,15},{2,12},{3,13},{4,10},{5,11},{6,8},{7,9},{8,6},{9,7},... | collective-permute-start | bytes 737288 | tf_op jit(solution)/shard_map/ppermute | solution.py:98
  172.3 37.0 %collective-permute-start.29 = (bf16[1,16,8,960]{3,2,1,0:T(8,128)(2,1)S(1)}, bf16[1,16,8,960]{3,2,1,0:T(8,128)(2,1)S(1)}, u32[]{:S(2)}, u32[]{:S(2)}) collective-permute-start(bf16[1,16,8,960]{3,2,1,0:T(8,128)(2,1)S(1)} %get-tuple-element.14), channel_id=1, source_target_pairs={{0,15},{1,14},{2,13},{3,12},{4,11},{5,10},{6,9},{7,8},{8,7},{9,6},... | collective-permute-start | bytes 737288 | tf_op jit(solution)/shard_map/ppermute | solution.py:98
  175.1 64.2 %slice-start = ((s8[6291456]{0:T(1024)(128)(4,1)}), s8[2097152]{0:T(1024)(128)(4,1)S(1)}, s32[]{:S(2)}) async-start(s8[6291456]{0:T(1024)(128)(4,1)} %bitcast.83), calls=%async_computation | async-start | bytes 4194304
  215.3 24.4 %collective-permute-start.30 = (bf16[1,16,8,384]{3,2,1,0:T(8,128)(2,1)S(1)}, bf16[1,16,8,384]{3,2,1,0:T(8,128)(2,1)S(1)}, u32[]{:S(2)}, u32[]{:S(2)}) collective-permute-start(bf16[1,16,8,384]{3,2,1,0:T(8,128)(2,1)S(1)} %get-tuple-element.44), channel_id=1, source_target_pairs={{0,1},{1,0},{2,3},{3,2},{4,5},{5,4},{6,7},{7,6},{8,9},{9,8},{10,11... | collective-permute-start | bytes 294920 | tf_op jit(solution)/shard_map/ppermute | solution.py:98
  215.7 24.0 %collective-permute-start.31 = (bf16[1,16,8,384]{3,2,1,0:T(8,128)(2,1)S(1)}, bf16[1,16,8,384]{3,2,1,0:T(8,128)(2,1)S(1)}, u32[]{:S(2)}, u32[]{:S(2)}) collective-permute-start(bf16[1,16,8,384]{3,2,1,0:T(8,128)(2,1)S(1)} %get-tuple-element.43), channel_id=1, source_target_pairs={{0,2},{1,3},{2,0},{3,1},{4,6},{5,7},{6,4},{7,5},{8,10},{9,11},{10,... | collective-permute-start | bytes 294920 | tf_op jit(solution)/shard_map/ppermute | solution.py:98
  215.7 26.8 %collective-permute-start.32 = (bf16[1,16,8,384]{3,2,1,0:T(8,128)(2,1)S(1)}, bf16[1,16,8,384]{3,2,1,0:T(8,128)(2,1)S(1)}, u32[]{:S(2)}, u32[]{:S(2)}) collective-permute-start(bf16[1,16,8,384]{3,2,1,0:T(8,128)(2,1)S(1)} %get-tuple-element.42), channel_id=1, source_target_pairs={{0,3},{1,2},{2,1},{3,0},{4,7},{5,6},{6,5},{7,4},{8,11},{9,10},{10,... | collective-permute-start | bytes 294920 | tf_op jit(solution)/shard_map/ppermute | solution.py:98
  217.5 25.2 %collective-permute-start.33 = (bf16[1,16,8,384]{3,2,1,0:T(8,128)(2,1)S(1)}, bf16[1,16,8,384]{3,2,1,0:T(8,128)(2,1)S(1)}, u32[]{:S(2)}, u32[]{:S(2)}) collective-permute-start(bf16[1,16,8,384]{3,2,1,0:T(8,128)(2,1)S(1)} %get-tuple-element.41), channel_id=1, source_target_pairs={{0,4},{1,5},{2,6},{3,7},{4,0},{5,1},{6,2},{7,3},{8,12},{9,13},{10,... | collective-permute-start | bytes 294920 | tf_op jit(solution)/shard_map/ppermute | solution.py:98
  217.5 27.8 %collective-permute-start.34 = (bf16[1,16,8,384]{3,2,1,0:T(8,128)(2,1)S(1)}, bf16[1,16,8,384]{3,2,1,0:T(8,128)(2,1)S(1)}, u32[]{:S(2)}, u32[]{:S(2)}) collective-permute-start(bf16[1,16,8,384]{3,2,1,0:T(8,128)(2,1)S(1)} %get-tuple-element.40), channel_id=1, source_target_pairs={{0,5},{1,4},{2,7},{3,6},{4,1},{5,0},{6,3},{7,2},{8,13},{9,12},{10,... | collective-permute-start | bytes 294920 | tf_op jit(solution)/shard_map/ppermute | solution.py:98
  219.2 20.0 %slice-start.1 = ((s8[6291456]{0:T(1024)(128)(4,1)}), s8[4194304]{0:T(1024)(128)(4,1)S(1)}, s32[]{:S(2)}) async-start(s8[6291456]{0:T(1024)(128)(4,1)} %bitcast.83), calls=%async_computation.1 | async-start | bytes 8388608
  239.6 5.8 %collective-permute-start.35 = (bf16[1,16,8,384]{3,2,1,0:T(8,128)(2,1)S(1)}, bf16[1,16,8,384]{3,2,1,0:T(8,128)(2,1)S(1)}, u32[]{:S(2)}, u32[]{:S(2)}) collective-permute-start(bf16[1,16,8,384]{3,2,1,0:T(8,128)(2,1)S(1)} %get-tuple-element.39), channel_id=1, source_target_pairs={{0,6},{1,7},{2,4},{3,5},{4,2},{5,3},{6,0},{7,1},{8,14},{9,15},{10,... | collective-permute-start | bytes 294920 | tf_op jit(solution)/shard_map/ppermute | solution.py:98
  239.8 9.3 %collective-permute-start.36 = (bf16[1,16,8,384]{3,2,1,0:T(8,128)(2,1)S(1)}, bf16[1,16,8,384]{3,2,1,0:T(8,128)(2,1)S(1)}, u32[]{:S(2)}, u32[]{:S(2)}) collective-permute-start(bf16[1,16,8,384]{3,2,1,0:T(8,128)(2,1)S(1)} %get-tuple-element.38), channel_id=1, source_target_pairs={{0,7},{1,6},{2,5},{3,4},{4,3},{5,2},{6,1},{7,0},{8,15},{9,14},{10,... | collective-permute-start | bytes 294920 | tf_op jit(solution)/shard_map/ppermute | solution.py:98
  242.5 6.7 %collective-permute-start.37 = (bf16[1,16,8,384]{3,2,1,0:T(8,128)(2,1)S(1)}, bf16[1,16,8,384]{3,2,1,0:T(8,128)(2,1)S(1)}, u32[]{:S(2)}, u32[]{:S(2)}) collective-permute-start(bf16[1,16,8,384]{3,2,1,0:T(8,128)(2,1)S(1)} %get-tuple-element.37), channel_id=1, source_target_pairs={{0,8},{1,9},{2,10},{3,11},{4,12},{5,13},{6,14},{7,15},{8,0},{9,1},... | collective-permute-start | bytes 294920 | tf_op jit(solution)/shard_map/ppermute | solution.py:98
  242.7 15.3 %collective-permute-start.38 = (bf16[1,16,8,384]{3,2,1,0:T(8,128)(2,1)S(1)}, bf16[1,16,8,384]{3,2,1,0:T(8,128)(2,1)S(1)}, u32[]{:S(2)}, u32[]{:S(2)}) collective-permute-start(bf16[1,16,8,384]{3,2,1,0:T(8,128)(2,1)S(1)} %get-tuple-element.36), channel_id=1, source_target_pairs={{0,9},{1,8},{2,11},{3,10},{4,13},{5,12},{6,15},{7,14},{8,1},{9,0},... | collective-permute-start | bytes 294920 | tf_op jit(solution)/shard_map/ppermute | solution.py:98
  245.3 16.9 %collective-permute-start.39 = (bf16[1,16,8,384]{3,2,1,0:T(8,128)(2,1)S(1)}, bf16[1,16,8,384]{3,2,1,0:T(8,128)(2,1)S(1)}, u32[]{:S(2)}, u32[]{:S(2)}) collective-permute-start(bf16[1,16,8,384]{3,2,1,0:T(8,128)(2,1)S(1)} %get-tuple-element.35), channel_id=1, source_target_pairs={{0,10},{1,11},{2,8},{3,9},{4,14},{5,15},{6,12},{7,13},{8,2},{9,3},... | collective-permute-start | bytes 294920 | tf_op jit(solution)/shard_map/ppermute | solution.py:98
  245.4 18.9 %collective-permute-start.40 = (bf16[1,16,8,384]{3,2,1,0:T(8,128)(2,1)S(1)}, bf16[1,16,8,384]{3,2,1,0:T(8,128)(2,1)S(1)}, u32[]{:S(2)}, u32[]{:S(2)}) collective-permute-start(bf16[1,16,8,384]{3,2,1,0:T(8,128)(2,1)S(1)} %get-tuple-element.34), channel_id=1, source_target_pairs={{0,11},{1,10},{2,9},{3,8},{4,15},{5,14},{6,13},{7,12},{8,3},{9,2},... | collective-permute-start | bytes 294920 | tf_op jit(solution)/shard_map/ppermute | solution.py:98
  249.1 23.1 %collective-permute-start.41 = (bf16[1,16,8,384]{3,2,1,0:T(8,128)(2,1)S(1)}, bf16[1,16,8,384]{3,2,1,0:T(8,128)(2,1)S(1)}, u32[]{:S(2)}, u32[]{:S(2)}) collective-permute-start(bf16[1,16,8,384]{3,2,1,0:T(8,128)(2,1)S(1)} %get-tuple-element.33), channel_id=1, source_target_pairs={{0,12},{1,13},{2,14},{3,15},{4,8},{5,9},{6,10},{7,11},{8,4},{9,5},... | collective-permute-start | bytes 294920 | tf_op jit(solution)/shard_map/ppermute | solution.py:98
  249.2 25.3 %collective-permute-start.42 = (bf16[1,16,8,384]{3,2,1,0:T(8,128)(2,1)S(1)}, bf16[1,16,8,384]{3,2,1,0:T(8,128)(2,1)S(1)}, u32[]{:S(2)}, u32[]{:S(2)}) collective-permute-start(bf16[1,16,8,384]{3,2,1,0:T(8,128)(2,1)S(1)} %get-tuple-element.32), channel_id=1, source_target_pairs={{0,13},{1,12},{2,15},{3,14},{4,9},{5,8},{6,11},{7,10},{8,5},{9,4},... | collective-permute-start | bytes 294920 | tf_op jit(solution)/shard_map/ppermute | solution.py:98
  258.0 17.8 %collective-permute-start.43 = (bf16[1,16,8,384]{3,2,1,0:T(8,128)(2,1)S(1)}, bf16[1,16,8,384]{3,2,1,0:T(8,128)(2,1)S(1)}, u32[]{:S(2)}, u32[]{:S(2)}) collective-permute-start(bf16[1,16,8,384]{3,2,1,0:T(8,128)(2,1)S(1)} %get-tuple-element.31), channel_id=1, source_target_pairs={{0,14},{1,15},{2,12},{3,13},{4,10},{5,11},{6,8},{7,9},{8,6},{9,7},... | collective-permute-start | bytes 294920 | tf_op jit(solution)/shard_map/ppermute | solution.py:98
  262.2 16.0 %collective-permute-start.44 = (bf16[1,16,8,384]{3,2,1,0:T(8,128)(2,1)S(1)}, bf16[1,16,8,384]{3,2,1,0:T(8,128)(2,1)S(1)}, u32[]{:S(2)}, u32[]{:S(2)}) collective-permute-start(bf16[1,16,8,384]{3,2,1,0:T(8,128)(2,1)S(1)} %get-tuple-element.30), channel_id=1, source_target_pairs={{0,15},{1,14},{2,13},{3,12},{4,11},{5,10},{6,9},{7,8},{8,7},{9,6},... | collective-permute-start | bytes 294920 | tf_op jit(solution)/shard_map/ppermute | solution.py:98
  (32 other events, 240.4 us)
